TPU v7x, 32 devices: a whole 2x2x4 slice. The times are simulated.
32 devices in a mesh: grp: 8 (over y, x, core), mem: 4 (over z).
Axes of the slice: x: 2, y: 2, z: 4, core: 2. Of those that a mesh axis runs over, the one named last changes fastest.
Arguments:
- points: float32 [16, 32768], P(None, ('grp', 'mem')), may hold values from -6 to 6
- residual: float32 [16, 32768], P(None, ('grp', 'mem')), may hold values from -6 to 6
- coef: float32 [16, 32768], P(None, ('grp', 'mem')), may hold values from -3 to 3
- block_of: int32 [32768], P(('grp', 'mem')), may hold values from 0 to 7, as said below
- order: int32 [2], replicated, may hold values from 0 to 7
- inverse: float32 [8, 4096, 4096], P('grp', 'mem'), may hold values from -1 to 2
Outputs:
- residual_out: float32 [16, 32768], P(None, ('grp', 'mem'))
- coef_out: float32 [16, 32768], P(None, ('grp', 'mem'))
Inputs may be any that keep to these rules, and one draw needn't show every extreme that they name: `block_of`: each run of 1024 consecutive points (the points of one device) holds exactly 128 points of every block.
All inputs are finite; a program needn't handle non-finite values.
Results may differ from a plain program's by a relative error of at most 0.00013.
Values sent between devices are 32-bit elements; how exact they have to be, the bound alone decides.
No kernel may reach another device: no remote copies, remote signals or barrier semaphores. Data moves between devices by JAX's collectives and lax.ppermute only.
A program may use at most 128 MiB of HBM per device.

v0:
```python
import jax
import jax.numpy as jnp
from jax import lax
from jax.sharding import PartitionSpec as P

B = 4096
STEPS = 2
ridge_weight = 0.5
kernel_scale = 0.125


def from_root(value, axis, source):
    kept = jnp.where(lax.axis_index(axis) == source, value, 0).astype(value.dtype)
    return lax.psum(kept, axis)


def body(points, residual, coef, block_of, order, inverse):
    highest = lax.Precision.HIGHEST
    n_mem = lax.axis_size("mem")
    per = B // (lax.axis_size("grp") * n_mem)
    slots = inverse.shape[0]
    mine = lax.axis_index("grp") * n_mem + lax.axis_index("mem")
    norms_local = jnp.sum(points * points, axis=0)
    for step_index in range(STEPS):
        block_id = order[step_index]
        inside = block_of == block_id
        position = jnp.cumsum(inside.astype(jnp.int32)) - 1
        select = (
            (position[:, None] == jnp.arange(per, dtype=jnp.int32)[None, :]) & inside[:, None]
        ).astype(jnp.float32)
        chosen_res = jnp.dot(residual, select, precision=highest)
        chosen_pts = jnp.dot(points, select, precision=highest)
        block_res, block_pts = (
            lax.all_gather(chosen_res, ("grp", "mem"), axis=1, tiled=True),
            lax.all_gather(chosen_pts, ("grp", "mem"), axis=1, tiled=True),
        )
        matrix_rows = lax.dynamic_index_in_dim(inverse, block_id % slots, 0, keepdims=False)
        solved = lax.dot_general(
            block_res, matrix_rows, (((1,), (1,)), ((), ())), precision=highest
        )
        owner = block_id // slots
        norms_block = jnp.sum(block_pts * block_pts, axis=0)
        assembled = lax.all_gather(solved, "mem", axis=1, tiled=True)
        assembled = from_root(assembled, "grp", owner)
        width = assembled.shape[1]
        cross = lax.dot_general(points, block_pts, (((0,), (0,)), ((), ())), precision=highest)
        kernel = jnp.exp(
            -kernel_scale * (norms_local[:, None] + norms_block[None, :] - 2.0 * cross)
        )
        total_update = lax.dot_general(
            assembled, kernel, (((1,), (1,)), ((), ())), precision=highest
        )
        ranks = jnp.arange(width, dtype=jnp.int32)
        wanted = mine * per + jnp.arange(per, dtype=jnp.int32)
        picker = (ranks[:, None] == wanted[None, :]).astype(jnp.float32)
        owned = jnp.dot(assembled, picker, precision=highest)
        update, owned = (total_update, owned)
        spread_back = lax.dot_general(owned, select, (((1,), (1,)), ((), ())), precision=highest)
        residual = residual - update - ridge_weight * spread_back
        coef = coef + spread_back
    return (residual, coef)


def solution(mesh):
    in_specs = (
        P(None, ("grp", "mem")),
        P(None, ("grp", "mem")),
        P(None, ("grp", "mem")),
        P(("grp", "mem")),
        P(),
        P("grp", "mem", None),
    )
    out_specs = (P(None, ("grp", "mem")), P(None, ("grp", "mem")))
    return jax.shard_map(body, mesh=mesh, in_specs=in_specs, out_specs=out_specs, check_vma=False)
```

profile of v0, /device:TPU:0, one launch (start us, length us, event | category | flops | bytes accessed | tf_op | source)
XLA Modules:
  0.0 461.2 jit_solution(17110810315561444372)
XLA Ops:
  7.2 1.3 fusion.67
  8.5 2.0 convert_bitcast_fusion
  10.5 0.3 reduce-window.16
  10.8 0.1 slice.21
  10.9 0.1 slice_reduce_fusion.1
  11.0 0.1 add_bitcast_fusion.1
  11.1 1.4 convolution_bitcast_fusion.2
  12.5 71.8 %all_gather.18 = f32[16,4096]{1,0:T(8,128)S(1)} all-gather(f32[16,128]{1,0:T(8,128)S(1)} %convolution_bitcast_fusion.2), channel_id=1, replica_groups=mesh['grp'=8,'mem'=4] {'grp','mem'}, dimensions={1}, use_global_device_ids=true | all-gather | bytes 270336 | tf_op jit(solution)/shard_map/all_gather | solution.py:34
  84.3 17.1 %fusion.10 = f32[16,1024]{1,0:T(8,128)S(1)} fusion(f32[16,4096]{1,0:T(8,128)S(1)} %all_gather.18, f32[1,1024,4096]{2,1,0:T(8,128)} %param.11), kind=kOutput, calls=%fused_computation.10 | convolution fusion | flops 805306368 | bytes 17104896 | tf_op jit(solution)/shard_map/dot_general | solution.py:38
  101.4 14.3 %all_gather.19 = f32[16,4096]{1,0:T(8,128)S(1)} all-gather(f32[16,1024]{1,0:T(8,128)S(1)} %fusion.10), channel_id=1, replica_groups=mesh['grp'=8,'mem'=4] {'mem'}, dimensions={1}, use_global_device_ids=true | all-gather | bytes 327680 | tf_op jit(solution)/shard_map/all_gather | solution.py:43
  116.4 0.7 broadcast_select_fusion.1
  117.2 0.5 convolution_bitcast_fusion.1
  117.7 65.6 %all_gather.20 = f32[16,4096]{1,0:T(8,128)S(1)} all-gather(f32[16,128]{1,0:T(8,128)S(1)} %convolution_bitcast_fusion.1), channel_id=1, replica_groups=mesh['grp'=8,'mem'=4] {'grp','mem'}, dimensions={1}, use_global_device_ids=true | all-gather | bytes 270336 | tf_op jit(solution)/shard_map/all_gather | solution.py:35
  183.3 15.9 %fusion.68 = f32[4096,1024]{1,0:T(8,128)} fusion(f32[16,4096]{1,0:T(8,128)S(1)} %all_gather.20, f32[16,1024]{1,0:T(8,128)S(1)} %copy-done), kind=kOutput, calls=%fused_computation.75 | convolution fusion | flops 805306368 | bytes 17104896 | tf_op jit(solution)/shard_map/dot_general | solution.py:46
  199.3 0.3 reduce-window.24
  199.6 0.1 slice_reduce_fusion
  199.8 0.1 add_bitcast_fusion
  199.8 0.5 convolution_bitcast_fusion
  201.0 67.7 %all_gather.23 = f32[16,4096]{1,0:T(8,128)S(1)} all-gather(f32[16,128]{1,0:T(8,128)S(1)} %convolution_bitcast_fusion), channel_id=1, replica_groups=mesh['grp'=8,'mem'=4] {'grp','mem'}, dimensions={1}, use_global_device_ids=true | all-gather | bytes 270336 | tf_op jit(solution)/shard_map/all_gather | solution.py:35
  268.7 1.7 fusion.25
  270.5 1.2 fusion.41
  271.6 14.8 %fusion.29 = f32[16,1024]{1,0:T(8,128)S(1)} fusion(f32[16,1024]{1,0:T(8,128)S(1)} %copy-done.1, f32[16,4096]{1,0:T(8,128)} %all-reduce.3.cloned.1.call-done, f32[4096,1024]{1,0:T(8,128)} %fusion.68, f32[4096]{0:T(1024)S(1)} %multiply_reduce_fusion.1, f32[1024]{0:T(1024)S(1)} %multiply_reduce_fusion.2, f32[16,1024]{1,0:T(8,128)S(1)} %fusion.41), kind=kOutput, calls=%fused_computation.28 | convolution fusion | flops 822132736 | bytes 17256448 | tf_op jit(solution)/shard_map/dot_general | solution.py:50
  286.4 0.5 fusion.49
  286.9 65.5 %all_gather.21 = f32[16,4096]{1,0:T(8,128)S(1)} all-gather(f32[16,128]{1,0:T(8,128)S(1)} %fusion.49), channel_id=1, replica_groups=mesh['grp'=8,'mem'=4] {'grp','mem'}, dimensions={1}, use_global_device_ids=true | all-gather | bytes 270336 | tf_op jit(solution)/shard_map/all_gather | solution.py:34
  352.4 17.2 %fusion.8 = f32[16,1024]{1,0:T(8,128)S(1)} fusion(f32[16,4096]{1,0:T(8,128)S(1)} %all_gather.21, f32[1,1024,4096]{2,1,0:T(8,128)} %param.11), kind=kOutput, calls=%fused_computation.8 | convolution fusion | flops 805306368 | bytes 17104896 | tf_op jit(solution)/shard_map/dot_general | solution.py:38
  369.6 14.3 %all_gather.22 = f32[16,4096]{1,0:T(8,128)S(1)} all-gather(f32[16,1024]{1,0:T(8,128)S(1)} %fusion.8), channel_id=1, replica_groups=mesh['grp'=8,'mem'=4] {'mem'}, dimensions={1}, use_global_device_ids=true | all-gather | bytes 327680 | tf_op jit(solution)/shard_map/all_gather | solution.py:43
  383.9 0.7 broadcast_select_fusion
  384.6 15.9 %fusion.69 = f32[4096,1024]{1,0:T(8,128)} fusion(f32[16,4096]{1,0:T(8,128)S(1)} %all_gather.23, f32[16,1024]{1,0:T(8,128)S(1)} %copy-done), kind=kOutput, calls=%fused_computation.76 | convolution fusion | flops 805306368 | bytes 17104896 | tf_op jit(solution)/shard_map/dot_general | solution.py:46
  400.6 35.4 %all-reduce.5.cloned.1.call-done = f32[16,4096]{1,0:T(8,128)} async-done(((f32[16,4096]{1,0:T(8,128)}), f32[16,4096]{1,0:T(8,128)}) %all-reduce.5.cloned.1.call-update) | async-done | bytes 262160 | tf_op jit(solution)/shard_map/psum | solution.py:14
  436.0 1.7 fusion.24
  437.8 1.2 add_add_fusion
  439.0 15.4 %fusion.35 = f32[16,1024]{1,0:T(8,128)} fusion(f32[16,1024]{1,0:T(8,128)S(1)} %fusion.29, f32[16,4096]{1,0:T(8,128)} %all-reduce.5.cloned.1.call-done, f32[4096,1024]{1,0:T(8,128)} %fusion.69, f32[4096]{0:T(1024)S(1)} %multiply_reduce_fusion, f32[1024]{0:T(1024)S(1)} %multiply_reduce_fusion.2, f32[16,1024]{1,0:T(8,128)S(1)} %get-tuple-element.11), kind=kOutput, calls=%fused_computation.30 | convolution fusion | flops 822132736 | bytes 17256448 | tf_op jit(solution)/shard_map/dot_general | solution.py:50
  (18 shorter events, 0.4 us)
Async XLA Ops:
  7.2 110.0 %copy-start = (f32[16,1024]{1,0:T(8,128)S(1)}, f32[16,1024]{1,0:T(8,128)}, u32[]{:S(2)}) copy-start(f32[16,1024]{1,0:T(8,128)} %param.6) | copy-start | bytes 196612
  7.2 261.5 %all-reduce.3.cloned.1.call-start = ((), (), s32[]{:S(2)}) async-start(), calls=%async_computation | async-start | bytes 524288 | tf_op jit(solution)/shard_map/psum | solution.py:14
  101.4 170.2 %copy-start.1 = (f32[16,1024]{1,0:T(8,128)S(1)}, f32[16,1024]{1,0:T(8,128)}, u32[]{:S(2)}) copy-start(f32[16,1024]{1,0:T(8,128)} %param.7) | copy-start | bytes 196612
  117.1 318.9 %all-reduce.5.cloned.1.call-start = ((), (), s32[]{:S(2)}) async-start(), calls=%async_computation.1 | async-start | bytes 524288 | tf_op jit(solution)/shard_map/psum | solution.py:14
  352.4 85.3 %copy-start.2 = (f32[16,1024]{1,0:T(8,128)S(1)}, f32[16,1024]{1,0:T(8,128)}, u32[]{:S(2)}) copy-start(f32[16,1024]{1,0:T(8,128)} %param.8) | copy-start | bytes 196612
Sparse Core Ops, SparseCore 0:
  117.3 49.9 all-reduce.2
  384.7 51.2 all-reduce.4
where the time goes:
time: 462 us; the launch traced here: 461 us
  blocking collectives  299 us (65%)
  matrix products  105 us (23%)
  waiting for transfers between devices  35.5 us (8%)
  between operations  15.5 us (3%)
    all_gather x2, blocking collectives, body(): lax.all_gather(chosen_res, ('grp', 'mem'), axis=1, tiled=True)  137 us
    all_gather x2, blocking collectives, body(): lax.all_gather(chosen_pts, ('grp', 'mem'), axis=1, tiled=True)  133 us
    psum x2, waiting for transfers between devices, from_root(): return lax.psum(kept, axis)  35.4 us
    dot_general x2, matrix products, body(): lax.dot_general(block_res, matrix_rows, (((1,), (1,)), ((), ())), precisi...  34.3 us
    dot_general x2, matrix products, body(): lax.dot_general(points, block_pts, (((0,), (0,)), ((), ())), precision=hi...  31.8 us
    dot_general x2, matrix products, body(): lax.dot_general(assembled, kernel, (((1,), (1,)), ((), ())), precision=hi...  30.2 us
    all_gather x2, blocking collectives, body(): assembled = lax.all_gather(solved, 'mem', axis=1, tiled=True)  28.6 us
  transfers between devices with their start and end apart: 2, of which 1 were waited for; matrix products, arithmetic and copies ran while one was open for 7% of the time, Pallas kernels for 0%

commit v1 on v0

--- a/solution.py
+++ b/solution.py
@@ -7,6 +7,18 @@
 STEPS = 2
 ridge_weight = 0.5
 kernel_scale = 0.125
+
+
+def gather_by_bits(x, axis, dim):
+    ways, here = (lax.axis_size(axis), lax.axis_index(axis))
+    grown, reach = (x, 1)
+    while reach < ways:
+        theirs = lax.ppermute(grown, axis, [(d, d ^ reach) for d in range(ways)])
+        mine_first = jnp.concatenate([grown, theirs], axis=dim)
+        theirs_first = jnp.concatenate([theirs, grown], axis=dim)
+        grown = jnp.where(here & reach == 0, mine_first, theirs_first)
+        reach = 2 * reach
+    return grown
 
 
 def from_root(value, axis, source):
@@ -31,7 +43,7 @@
         chosen_res = jnp.dot(residual, select, precision=highest)
         chosen_pts = jnp.dot(points, select, precision=highest)
         block_res, block_pts = (
-            lax.all_gather(chosen_res, ("grp", "mem"), axis=1, tiled=True),
+            gather_by_bits(chosen_res, ("grp", "mem"), 1),
             lax.all_gather(chosen_pts, ("grp", "mem"), axis=1, tiled=True),
         )
         matrix_rows = lax.dynamic_index_in_dim(inverse, block_id % slots, 0, keepdims=False)

time: 462 us -> 426 us (0.922); the launches traced: 461 us -> 417 us
  blocking collectives: 299 us -> 164 us
  waiting for transfers between devices: 35.5 us -> 90.9 us
  starting transfers between devices: 0.08 us -> 24.5 us
  matrix products: 105 us -> 116 us
    all_gather x2 -> x0, blocking collectives: 137 us -> none  [body(): lax.all_gather(chosen_res, ('grp', 'mem'), axis=1, tiled=True)]
    psum x2, waiting for transfers between devices: 35.4 us -> 74.3 us  [from_root(): return lax.psum(kept, axis)]
    ppermute x0 -> x10, waiting for transfers between devices: none -> 16.6 us  [gather_by_bits(): theirs = lax.ppermute(grown, axis, [(d, d ^ reach) for d in range(ways)])]
    ppermute x0 -> x10, starting transfers between devices: none -> 13.5 us  [gather_by_bits(): theirs = lax.ppermute(grown, axis, [(d, d ^ reach) for d in range(ways)])]
    psum x2, starting transfers between devices: 0.08 us -> 11 us  [from_root(): return lax.psum(kept, axis)]
    dot_general x2, matrix products: 30.2 us -> 39.4 us  [body(): lax.dot_general(assembled, kernel, (((1,), (1,)), ((), ())), precision=hi...]
  transfers between devices with their start and end apart: 2 -> 12, of which waited for: 1 -> 9; matrix products, arithmetic and copies ran while one was open for 7% -> 8% of each run, Pallas kernels for 0% -> 0%
where the time goes in v1:
time: 426 us; the launch traced here: 417 us
  blocking collectives  164 us (38%)
  matrix products  116 us (27%)
  waiting for transfers between devices  90.9 us (21%)
  starting transfers between devices  24.5 us (6%)
  between operations  15.9 us (4%)
  other arithmetic  4.35 us (1%)
    all_gather x2, blocking collectives, body(): lax.all_gather(chosen_pts, ('grp', 'mem'), axis=1, tiled=True)  135 us
    psum x2, waiting for transfers between devices, from_root(): return lax.psum(kept, axis)  74.3 us
    dot_general x2, matrix products, body(): lax.dot_general(assembled, kernel, (((1,), (1,)), ((), ())), precision=hi...  39.4 us
    dot_general x2, matrix products, body(): lax.dot_general(block_res, matrix_rows, (((1,), (1,)), ((), ())), precisi...  34.6 us
    dot_general x2, matrix products, body(): lax.dot_general(points, block_pts, (((0,), (0,)), ((), ())), precision=hi...  32.4 us
    all_gather x2, blocking collectives, body(): assembled = lax.all_gather(solved, 'mem', axis=1, tiled=True)  28.6 us
    ppermute x10, waiting for transfers between devices, gather_by_bits(): theirs = lax.ppermute(grown, axis, [(d, d ^ reach) for d in range(ways)])  16.6 us
    ppermute x10, starting transfers between devices, gather_by_bits(): theirs = lax.ppermute(grown, axis, [(d, d ^ reach) for d in range(ways)])  13.5 us
  transfers between devices with their start and end apart: 12, of which 9 were waited for; matrix products, arithmetic and copies ran while one was open for 8% of the time, Pallas kernels for 0%

profile of v1, /device:TPU:0, one launch (start us, length us, event | category | flops | bytes accessed | tf_op | source)
XLA Modules:
  0.0 417.1 jit_solution(17333382219469734317)
XLA Ops:
  7.2 1.3 fusion.81
  8.5 2.0 convert_bitcast_fusion
  11.1 1.4 convolution_bitcast_fusion.2
  12.4 3.1 collective-permute-start
  15.5 1.4 convolution_bitcast_fusion.1
  17.2 3.0 collective-permute-start.1
  20.2 67.0 %all_gather.13 = f32[16,4096]{1,0:T(8,128)S(1)} all-gather(f32[16,128]{1,0:T(8,128)S(1)} %convolution_bitcast_fusion.1), channel_id=1, replica_groups=mesh['grp'=8,'mem'=4] {'grp','mem'}, dimensions={1}, use_global_device_ids=true | all-gather | bytes 270336 | tf_op jit(solution)/shard_map/all_gather | solution.py:47
  87.3 16.6 %fusion.82 = f32[4096,1024]{0,1:T(8,128)} fusion(f32[16,4096]{1,0:T(8,128)S(1)} %all_gather.13, f32[16,1024]{1,0:T(8,128)} %param.6), kind=kOutput, calls=%fused_computation.99 | convolution fusion | flops 805306368 | bytes 17104896 | tf_op jit(solution)/shard_map/dot_general | solution.py:58
  104.5 4.4 %collective-permute-done.3 = f32[16,1024]{1,0:T(8,128)S(1)} collective-permute-done((f32[16,1024]{1,0:T(8,128)S(1)}, f32[16,1024]{1,0:T(8,128)S(1)}, u32[]{:S(2)}, u32[]{:S(2)}) %collective-permute-start.3) | collective-permute-done | bytes 65568 | tf_op jit(solution)/shard_map/ppermute | solution.py:16
  108.9 1.5 collective-permute-start.4
  111.1 2.9 collective-permute-done.4
  114.1 17.3 %fusion.10 = f32[16,1024]{1,0:T(8,128)S(1)} fusion(f32[1,1024,4096]{2,1,0:T(8,128)} %param.11, f32[16,2048]{1,0:T(8,128)S(1)} %collective-permute-done.4, f32[16,2048]{1,0:T(8,128)S(1)} %maximum_select_fusion.4, pred[]{:T(512)S(6)} %eq.44), kind=kOutput, calls=%fused_computation.10 | convolution fusion | flops 805502976 | bytes 17104896 | tf_op jit(solution)/shard_map/dot_general | solution.py:50
  131.3 14.0 %all_gather.12 = f32[16,4096]{1,0:T(8,128)S(1)} all-gather(f32[16,1024]{1,0:T(8,128)S(1)} %fusion.10), channel_id=1, replica_groups=mesh['grp'=8,'mem'=4] {'mem'}, dimensions={1}, use_global_device_ids=true | all-gather | bytes 327680 | tf_op jit(solution)/shard_map/all_gather | solution.py:55
  146.0 11.0 %all-reduce.5.cloned.1.call-start = ((), (), s32[]{:S(2)}) async-start(), calls=%async_computation.1 | async-start | bytes 524288 | tf_op jit(solution)/shard_map/psum | solution.py:26
  157.1 40.1 %all-reduce.3.cloned.1.call-done = f32[16,4096]{1,0:T(8,128)} async-done(((f32[16,4096]{1,0:T(8,128)}), f32[16,4096]{1,0:T(8,128)}) %all-reduce.3.cloned.1.call-update) | async-done | bytes 262160 | tf_op jit(solution)/shard_map/psum | solution.py:26
  197.2 1.7 fusion.25
  198.9 1.2 fusion.41
  200.1 19.4 %fusion.29 = f32[16,1024]{1,0:T(8,128)S(1)} fusion(f32[16,1024]{1,0:T(8,128)S(1)} %copy-done.1, f32[16,4096]{1,0:T(8,128)} %all-reduce.3.cloned.1.call-done, f32[4096,1024]{0,1:T(8,128)} %fusion.82, f32[4096]{0:T(1024)S(1)} %multiply_reduce_fusion.1, f32[1024]{0:T(1024)S(1)} %multiply_reduce_fusion.2, f32[16,1024]{1,0:T(8,128)S(1)} %fusion.41), kind=kOutput, calls=%fused_computation.28 | convolution fusion | flops 822132736 | bytes 17256448 | tf_op jit(solution)/shard_map/dot_general | solution.py:62
  220.1 1.6 collective-permute-start.5
  221.6 2.2 collective-permute-done.5
  223.8 2.4 collective-permute-start.6
  226.2 2.2 collective-permute-done.6
  228.4 1.2 collective-permute-done.7
  230.5 3.4 collective-permute-done.8
  236.1 68.2 %all_gather.15 = f32[16,4096]{1,0:T(8,128)S(1)} all-gather(f32[16,128]{1,0:T(8,128)S(1)} %convolution_bitcast_fusion), channel_id=1, replica_groups=mesh['grp'=8,'mem'=4] {'grp','mem'}, dimensions={1}, use_global_device_ids=true | all-gather | bytes 270336 | tf_op jit(solution)/shard_map/all_gather | solution.py:47
  304.2 17.3 %fusion.8 = f32[16,1024]{1,0:T(8,128)S(1)} fusion(f32[1,1024,4096]{2,1,0:T(8,128)} %param.11, f32[16,2048]{1,0:T(8,128)S(1)} %collective-permute-done.9, f32[16,2048]{1,0:T(8,128)S(1)} %maximum_select_fusion.5, pred[]{:T(512)S(6)} %eq.44), kind=kOutput, calls=%fused_computation.8 | convolution fusion | flops 805502976 | bytes 17104896 | tf_op jit(solution)/shard_map/dot_general | solution.py:50
  321.5 14.6 %all_gather.14 = f32[16,4096]{1,0:T(8,128)S(1)} all-gather(f32[16,1024]{1,0:T(8,128)S(1)} %fusion.8), channel_id=1, replica_groups=mesh['grp'=8,'mem'=4] {'mem'}, dimensions={1}, use_global_device_ids=true | all-gather | bytes 327680 | tf_op jit(solution)/shard_map/all_gather | solution.py:55
  336.8 15.8 %fusion.83 = f32[4096,1024]{0,1:T(8,128)} fusion(f32[16,4096]{1,0:T(8,128)S(1)} %all_gather.15, f32[16,1024]{1,0:T(8,128)S(1)} %copy-done), kind=kOutput, calls=%fused_computation.100 | convolution fusion | flops 805306368 | bytes 17104896 | tf_op jit(solution)/shard_map/dot_general | solution.py:58
  352.7 34.2 %all-reduce.5.cloned.1.call-done = f32[16,4096]{1,0:T(8,128)} async-done(((f32[16,4096]{1,0:T(8,128)}), f32[16,4096]{1,0:T(8,128)}) %all-reduce.5.cloned.1.call-update) | async-done | bytes 262160 | tf_op jit(solution)/shard_map/psum | solution.py:26
  386.9 1.7 fusion.24
  388.7 1.2 add_add_fusion
  389.9 20.0 %fusion.35 = f32[16,1024]{1,0:T(8,128)} fusion(f32[16,1024]{1,0:T(8,128)S(1)} %fusion.29, f32[16,4096]{1,0:T(8,128)} %all-reduce.5.cloned.1.call-done, f32[4096,1024]{0,1:T(8,128)} %fusion.83, f32[4096]{0:T(1024)S(1)} %multiply_reduce_fusion, f32[1024]{0:T(1024)S(1)} %multiply_reduce_fusion.2, f32[16,1024]{1,0:T(8,128)S(1)} %get-tuple-element.11), kind=kOutput, calls=%fused_computation.30 | convolution fusion | flops 822132736 | bytes 17256448 | tf_op jit(solution)/shard_map/dot_general | solution.py:62
  (44 shorter events, 6.1 us)
Async XLA Ops:
  7.2 103.9 %copy-start = (f32[16,1024]{1,0:T(8,128)S(1)}, f32[16,1024]{1,0:T(8,128)}, u32[]{:S(2)}) copy-start(f32[16,1024]{1,0:T(8,128)} %param.6) | copy-start | bytes 196612
  7.2 190.0 %all-reduce.3.cloned.1.call-start = ((), (), s32[]{:S(2)}) async-start(), calls=%async_computation | async-start | bytes 524288 | tf_op jit(solution)/shard_map/psum | solution.py:26
  12.4 4.7 %collective-permute-start = (f32[16,128]{1,0:T(8,128)S(1)}, f32[16,128]{1,0:T(8,128)S(1)}, u32[]{:S(2)}, u32[]{:S(2)}) collective-permute-start(f32[16,128]{1,0:T(8,128)S(1)} %convolution_bitcast_fusion.2), channel_id=1, source_target_pairs={{0,1},{1,0},{2,3},{3,2},{4,5},{5,4},{6,7},{7,6},{8,9},{9,8},{10,11... | collective-permute-start | bytes 24584 | tf_op jit(solution)/shard_map/ppermute | solution.py:16
  17.2 70.1 %collective-permute-start.1 = (f32[16,256]{1,0:T(8,128)S(1)}, f32[16,256]{1,0:T(8,128)S(1)}, u32[]{:S(2)}, u32[]{:S(2)}) collective-permute-start(f32[16,256]{1,0:T(8,128)S(1)} %maximum_select_fusion.10), channel_id=1, source_target_pairs={{0,2},{1,3},{2,0},{3,1},{4,6},{5,7},{6,4},{7,5},{8,10},{9,11},{10,... | collective-permute-start | bytes 49160 | tf_op jit(solution)/shard_map/ppermute | solution.py:16
  87.2 112.8 %copy-start.1 = (f32[16,1024]{1,0:T(8,128)S(1)}, f32[16,1024]{1,0:T(8,128)}, u32[]{:S(2)}) copy-start(f32[16,1024]{1,0:T(8,128)} %param.7) | copy-start | bytes 196612
  87.3 17.0 %collective-permute-start.2 = (f32[16,512]{1,0:T(8,128)S(1)}, f32[16,512]{1,0:T(8,128)S(1)}, u32[]{:S(2)}, u32[]{:S(2)}) collective-permute-start(f32[16,512]{1,0:T(8,128)S(1)} %maximum_select_fusion.8), channel_id=1, source_target_pairs={{0,4},{1,5},{2,6},{3,7},{4,0},{5,1},{6,2},{7,3},{8,12},{9,13},{10,... | collective-permute-start | bytes 98312 | tf_op jit(solution)/shard_map/ppermute | solution.py:16
  104.3 4.6 %collective-permute-start.3 = (f32[16,1024]{1,0:T(8,128)S(1)}, f32[16,1024]{1,0:T(8,128)S(1)}, u32[]{:S(2)}, u32[]{:S(2)}) collective-permute-start(f32[16,1024]{1,0:T(8,128)S(1)} %maximum_select_fusion.6), channel_id=1, source_target_pairs={{0,8},{1,9},{2,10},{3,11},{4,12},{5,13},{6,14},{7,15},{8,0},{9,1},... | collective-permute-start | bytes 196616 | tf_op jit(solution)/shard_map/ppermute | solution.py:16
  108.9 5.2 %collective-permute-start.4 = (f32[16,2048]{1,0:T(8,128)S(1)}, f32[16,2048]{1,0:T(8,128)S(1)}, u32[]{:S(2)}, u32[]{:S(2)}) collective-permute-start(f32[16,2048]{1,0:T(8,128)S(1)} %maximum_select_fusion.4), channel_id=1, source_target_pairs={{0,16},{1,17},{2,18},{3,19},{4,20},{5,21},{6,22},{7,23},{8,24},{9,... | collective-permute-start | bytes 393224 | tf_op jit(solution)/shard_map/ppermute | solution.py:16
  146.0 240.9 %all-reduce.5.cloned.1.call-start = ((), (), s32[]{:S(2)}) async-start(), calls=%async_computation.1 | async-start | bytes 524288 | tf_op jit(solution)/shard_map/psum | solution.py:26
  220.1 3.7 collective-permute-start.5
  223.8 4.6 %collective-permute-start.6 = (f32[16,256]{1,0:T(8,128)S(1)}, f32[16,256]{1,0:T(8,128)S(1)}, u32[]{:S(2)}, u32[]{:S(2)}) collective-permute-start(f32[16,256]{1,0:T(8,128)S(1)} %maximum_select_fusion.11), channel_id=1, source_target_pairs={{0,2},{1,3},{2,0},{3,1},{4,6},{5,7},{6,4},{7,5},{8,10},{9,11},{10,... | collective-permute-start | bytes 49160 | tf_op jit(solution)/shard_map/ppermute | solution.py:16
  228.4 1.2 collective-permute-start.7
  229.6 4.3 %collective-permute-start.8 = (f32[16,1024]{1,0:T(8,128)S(1)}, f32[16,1024]{1,0:T(8,128)S(1)}, u32[]{:S(2)}, u32[]{:S(2)}) collective-permute-start(f32[16,1024]{1,0:T(8,128)S(1)} %maximum_select_fusion.7), channel_id=1, source_target_pairs={{0,8},{1,9},{2,10},{3,11},{4,12},{5,13},{6,14},{7,15},{8,0},{9,1},... | collective-permute-start | bytes 196616 | tf_op jit(solution)/shard_map/ppermute | solution.py:16
  234.0 70.2 %collective-permute-start.9 = (f32[16,2048]{1,0:T(8,128)S(1)}, f32[16,2048]{1,0:T(8,128)S(1)}, u32[]{:S(2)}, u32[]{:S(2)}) collective-permute-start(f32[16,2048]{1,0:T(8,128)S(1)} %maximum_select_fusion.5), channel_id=1, source_target_pairs={{0,16},{1,17},{2,18},{3,19},{4,20},{5,21},{6,22},{7,23},{8,24},{9,... | collective-permute-start | bytes 393224 | tf_op jit(solution)/shard_map/ppermute | solution.py:16
  304.2 84.5 %copy-start.2 = (f32[16,1024]{1,0:T(8,128)S(1)}, f32[16,1024]{1,0:T(8,128)}, u32[]{:S(2)}) copy-start(f32[16,1024]{1,0:T(8,128)} %param.8) | copy-start | bytes 196612
Sparse Core Ops, SparseCore 0:
  146.2 50.9 all-reduce.2
  337.0 49.9 all-reduce.4
